TPU v7x, 32 devices: a whole 2x2x4 slice. The times are simulated.
32 devices in a mesh: groups: 2 (over y), wide: 4 (over z), ctx: 4 (over x, core).
Axes of the slice: x: 2, y: 2, z: 4, core: 2. Of those that a mesh axis runs over, the one named last changes fastest.
Arguments:
- queries: bfloat16 [4096, 6144], P(('groups', 'ctx'), 'wide'), parts along dimension 0, may hold values from -48 to 48
- key_rows: bfloat16 [4096, 1024], P(('groups', 'ctx')), parts along dimension 0, may hold values from -48 to 48
- value_head_rows: bfloat16 [4096, 1024], P(('groups', 'ctx')), parts along dimension 0, may hold values from -18 to 18
- residual: bfloat16 [4096, 6144], P(('groups', 'ctx'), 'wide'), parts along dimension 0, may hold values from -48 to 48
- out_weight: bfloat16 [6144, 6144], P('wide'), may hold values from -0.109375 to 0.109375
- norm_gain: bfloat16 [6144], P('wide'), may hold values from 0.25 to 1.75
- router_weight: bfloat16 [6144, 8], P('wide'), may hold values from -0.078125 to 0.078125
- gate_weight: bfloat16 [6144, 8192], P('wide', 'ctx'), may hold values from -0.078125 to 0.078125
- up_weight: bfloat16 [6144, 8192], P('wide', 'ctx'), may hold values from -0.078125 to 0.078125
- down_weight: bfloat16 [8192, 6144], P('ctx', 'wide'), may hold values from -0.0625 to 0.0625
- expert_ids: int32 [4096, 2], P('groups'), parts along dimension 0, may hold values from 0 to 7, as said below
- slot_ids: int32 [4096, 2], P('groups'), parts along dimension 0, may hold values from -1 to 639, as said below
Outputs:
- layer_out: bfloat16 [4096, 6144], P(('groups', 'ctx'), 'wide'), parts along dimension 0
There are 2 independent parts, one for each index of `groups`. A program takes and returns all parts, laid end to end along the dimension named above; an argument that names none is the same for every part. Nothing has to cross between parts.
Inputs may be any that keep to these rules, and one draw needn't show every extreme that they name: `expert_ids`: each row names 2 different experts; expert 0 is named by at least 704 rows, so its buffer is full in every draw. `slot_ids`: the rows naming one expert take its buffer rows 0, 1, 2 and so on in the order of positions (for one position, the earlier column first); once 640 rows are taken, further choices of that expert hold -1. Rows of one expert's buffer are never shared.
All inputs are finite; a program needn't handle non-finite values.
Results may differ from a plain program's by a relative error of at most 0.015.
Values may be sent and summed in bfloat16 or wider, within the bound.
No kernel may reach another device: no remote copies, remote signals or barrier semaphores. Data moves between devices by JAX's collectives and lax.ppermute only.
A program may use at most 192 MiB of HBM per device.

v0:
```python
import math
import jax
import jax.numpy as jnp
from jax import lax
from jax.sharding import PartitionSpec as P

D = 6144
QUERY_HEADS = 48
KEY_VALUE_HEADS = 8
HEAD_SIZE = 128
NEG_FILL = -1e30
EPSILON = 1e-05


def token_slots(expert_ids, slot_ids, capacity):
    in_window = jnp.logical_and(expert_ids == 0, slot_ids >= 0)
    picked = jnp.max(jnp.where(in_window, slot_ids, -1), axis=1)
    return jnp.where(picked >= 0, picked, capacity)


def other_experts(expert_ids, slot_of_token, capacity):
    partner = jnp.sum(expert_ids, axis=1)
    return jnp.zeros((capacity,), jnp.int32).at[slot_of_token].set(partner, mode="drop")


def expert_hidden(gate_sum, up_sum, square_sum, logit_sum, slot_other, model_width):
    inverse_rms = lax.rsqrt(square_sum / model_width + EPSILON)
    gate_value = gate_sum * inverse_rms[:, None]
    up_value = up_sum * inverse_rms[:, None]
    logit_value = logit_sum * inverse_rms[:, None]
    columns = jnp.arange(logit_value.shape[1], dtype=jnp.int32)
    partner_logit = jnp.sum(
        jnp.where(columns[None, :] == slot_other[:, None], logit_value, 0.0), axis=1
    )
    mixing = jax.nn.sigmoid(logit_value[:, 0] - partner_logit)
    return (jax.nn.silu(gate_value) * up_value * mixing[:, None]).astype(jnp.bfloat16)


def local(
    queries,
    key_rows,
    value_head_rows,
    residual,
    out_weight,
    norm_gain,
    router_weight,
    gate_weight,
    up_weight,
    down_weight,
    expert_ids,
    slot_ids,
):
    ctx_count = lax.axis_size("ctx")
    wide_index = lax.axis_index("wide")
    ctx_index = lax.axis_index("ctx")
    rows_local = queries.shape[0]
    heads_local = queries.shape[1] // HEAD_SIZE
    query_group_width = QUERY_HEADS // KEY_VALUE_HEADS
    shared_heads = max(1, heads_local // query_group_width)
    per_shared = heads_local // shared_heads
    first_shared = wide_index * heads_local // query_group_width
    key_used = lax.dynamic_slice_in_dim(
        key_rows, first_shared * HEAD_SIZE, shared_heads * HEAD_SIZE, 1
    )
    value_used = lax.dynamic_slice_in_dim(
        value_head_rows, first_shared * HEAD_SIZE, shared_heads * HEAD_SIZE, 1
    )
    query_blocks = queries.reshape(rows_local, shared_heads, per_shared, HEAD_SIZE)
    query_pos = ctx_index * rows_local + jnp.arange(rows_local, dtype=jnp.int32)
    last_query = ctx_index * rows_local + rows_local - 1
    scale_factor = 1.0 / math.sqrt(HEAD_SIZE)
    start_state = (
        jnp.full((shared_heads, per_shared, rows_local), -jnp.inf, jnp.float32),
        jnp.zeros((shared_heads, per_shared, rows_local), jnp.float32),
        jnp.zeros((shared_heads, per_shared, rows_local, HEAD_SIZE), jnp.float32),
    )
    pieces = (
        lax.all_gather(key_used, "ctx", axis=0, tiled=True),
        lax.all_gather(value_used, "ctx", axis=0, tiled=True),
    )

    def update(state):
        running_max, running_sum, running_acc = state
        key_piece = pieces[0].reshape(-1, shared_heads, HEAD_SIZE)
        value_piece = pieces[1].reshape(-1, shared_heads, HEAD_SIZE)
        scores = (
            jnp.einsum(
                "skqd,rkd->kqsr", query_blocks, key_piece, preferred_element_type=jnp.float32
            )
            * scale_factor
        )
        key_pos = jnp.arange(key_piece.shape[0], dtype=jnp.int32)
        allowed = (key_pos[None, :] <= query_pos[:, None])[None, None, :, :]
        masked = jnp.where(allowed, scores, NEG_FILL)
        new_max = jnp.max(masked, axis=-1)
        weights = jnp.where(allowed, jnp.exp(masked - new_max[..., None]), 0.0)
        decay = jnp.exp(running_max - new_max)
        new_sum = running_sum * decay + jnp.sum(weights, axis=-1)
        added = jnp.einsum(
            "kqsr,rkd->kqsd",
            weights.astype(jnp.bfloat16),
            value_piece,
            preferred_element_type=jnp.float32,
        )
        return (new_max, new_sum, running_acc * decay[..., None] + added)

    final_max, final_sum, final_acc = lax.cond(
        jnp.int32(0) > last_query, lambda state: state, update, start_state
    )
    attended = final_acc / final_sum[..., None]
    attended = (
        jnp.transpose(attended, (2, 0, 1, 3))
        .reshape(rows_local, heads_local * HEAD_SIZE)
        .astype(jnp.bfloat16)
    )
    partial_out = jnp.dot(attended, out_weight, preferred_element_type=jnp.float32)
    head_sum = lax.psum_scatter(
        partial_out.astype(jnp.bfloat16), "wide", scatter_dimension=1, tiled=True
    ).astype(jnp.float32)
    resid = (residual.astype(jnp.float32) + head_sum).astype(jnp.bfloat16)
    seq_len = rows_local * ctx_count
    capacity = seq_len * 5 // 16
    width_local = resid.shape[1]
    slot_of_token = token_slots(expert_ids, slot_ids, capacity)
    slot_other = other_experts(expert_ids, slot_of_token, capacity)
    buffer = (
        jnp.zeros((capacity, width_local), jnp.bfloat16)
        .at[slot_of_token]
        .set(lax.all_gather(resid, "ctx", axis=0, tiled=True), mode="drop")
    )
    buffer_wide = buffer.astype(jnp.float32)
    square_part = jnp.sum(buffer_wide * buffer_wide, axis=1)
    scaled = (buffer_wide * norm_gain.astype(jnp.float32)[None, :]).astype(jnp.bfloat16)
    gate_part = jnp.dot(scaled, gate_weight, preferred_element_type=jnp.float32)
    up_part = jnp.dot(scaled, up_weight, preferred_element_type=jnp.float32)
    logit_part = jnp.dot(scaled, router_weight, preferred_element_type=jnp.float32)
    gate_sum, up_sum, square_sum, logit_sum = (
        lax.psum(gate_part.astype(jnp.bfloat16), "wide").astype(jnp.float32),
        lax.psum(up_part.astype(jnp.bfloat16), "wide").astype(jnp.float32),
        lax.psum(square_part.astype(jnp.bfloat16), "wide").astype(jnp.float32),
        lax.psum(logit_part.astype(jnp.bfloat16), "wide").astype(jnp.float32),
    )
    hidden = expert_hidden(gate_sum, up_sum, square_sum, logit_sum, slot_other, D)
    expert_part = jnp.dot(hidden, down_weight, preferred_element_type=jnp.float32)
    expert_pad = jnp.concatenate([expert_part, jnp.zeros((1, width_local), jnp.float32)], axis=0)
    moe_rows = lax.psum_scatter(
        jnp.take(expert_pad, slot_of_token, axis=0).astype(jnp.bfloat16),
        "ctx",
        scatter_dimension=0,
        tiled=True,
    ).astype(jnp.float32)
    return (resid.astype(jnp.float32) + moe_rows).astype(jnp.bfloat16)


def solution(mesh):
    placed = (
        P(("groups", "ctx"), "wide"),
        P(("groups", "ctx"), None),
        P(("groups", "ctx"), None),
        P(("groups", "ctx"), "wide"),
        P("wide", None),
        P("wide"),
        P("wide", None),
        P("wide", "ctx"),
        P("wide", "ctx"),
        P("ctx", "wide"),
        P("groups", None),
        P("groups", None),
    )
    return jax.shard_map(
        local, mesh=mesh, in_specs=placed, out_specs=P(("groups", "ctx"), "wide"), check_vma=False
    )
```

profile of v0, /device:TPU:0, one launch (start us, length us, event | category | flops | bytes accessed | tf_op | source)
XLA Modules:
  0.0 613.0 jit_solution(8369827461181199514)
XLA Ops:
  6.5 1.2 copy-done
  7.8 0.7 constant_dynamic-slice_fusion.1
  8.5 0.0 all-gather.4.cloned.1.call-update
  8.5 0.0 all-gather.6.cloned.1.call-start
  8.6 1.7 constant_dynamic-slice_fusion
  10.2 0.0 all-gather.6.cloned.1.call-update
  10.3 0.0 reduce-scatter.3.cloned.1.call-start
  10.3 18.0 %all-gather.4.cloned.1.call-done = bf16[2048,256]{1,0:T(8,128)(2,1)} async-done(((bf16[512,256]{1,0:T(8,128)(2,1)}), bf16[2048,256]{1,0:T(8,128)(2,1)}) %all-gather.4.cloned.1.call-update) | async-done | bytes 1048592 | tf_op jit(solution)/shard_map/all_gather | solution.py:78
  28.3 18.3 %all-gather.6.cloned.1.call-done = bf16[2048,256]{1,0:T(8,128)(2,1)} async-done(((bf16[512,256]{1,0:T(8,128)(2,1)}), bf16[2048,256]{1,0:T(8,128)(2,1)}) %all-gather.6.cloned.1.call-update) | async-done | bytes 1048592 | tf_op jit(solution)/shard_map/all_gather | solution.py:79
  46.6 75.7 %conditional.1 = (f32[2,6,512]{2,1,0:T(8,128)S(1)}, f32[2,6,512,128]{2,3,1,0:T(8,128)}) conditional(s32[]{:T(128)} %convert_element_type.76, (s32[]{:T(128)}, s32[512]{0:T(512)S(1)}, bf16[2048,256]{1,0:T(8,128)(2,1)}, bf16[512,1536]{1,0:T(8,128)(2,1)}, bf16[2048,256]{1,0:T(8,128)(2,1)}) %tuple.13, () %tuple.14), branch_computations={%region_0.3_spmd, %region_3.4_spmd} | conditional | flops 6607870464 | bytes 180058160 | solution.py:107
  46.6 0.8 iota_compare_fusion
  47.5 1.7 copy.28
  49.2 2.1 reshape.71
  51.3 21.1 %fusion = (f32[2,6,512]{2,1,0:T(8,128)S(1)}, f32[2,2048,512,6]{2,1,3,0:T(8,128)}) fusion(pred[512,2048]{0,1:T(8,128)(4,1)S(1)} %iota_compare_fusion, bf16[512,2,6,128]{0,3,2,1:T(8,128)(2,1)S(1)} %bitcast.29, bf16[2048,2,128,1]{2,1,0,3:T(2,128)(2,1)} %bitcast.30), kind=kOutput, calls=%fused_computation.5 | convolution fusion | flops 3258968064 | bytes 54026240 | tf_op jit(solution)/shard_map/cond/branch_0_fun/skqd,rkd->kqsr/dot_general | solution.py:87
  72.4 22.0 %fusion.2 = f32[2,6,512]{2,1,0:T(8,128)S(1)} fusion(f32[2,2048,512,6]{2,1,3,0:T(8,128)} %get-tuple-element.49, f32[2,6,512]{2,1,0:T(8,128)S(1)} %get-tuple-element.48, pred[512,2048]{0,1:T(8,128)(4,1)S(1)} %iota_compare_fusion), kind=kLoop, calls=%fused_computation.7 | loop fusion | flops 62908416 | bytes 51429376 | tf_op jit(solution)/shard_map/cond/branch_0_fun/reduce_sum | solution.py:98
  94.4 0.3 reshape.73
  94.7 24.0 %fusion.6 = f32[2,6,512,128]{3,2,1,0:T(8,128)} fusion(f32[2,2048,512,6]{2,1,3,0:T(8,128)} %get-tuple-element.49, f32[2,6,512]{2,1,0:T(8,128)S(1)} %get-tuple-element.48, pred[512,2048]{0,1:T(8,128)(4,1)S(1)} %iota_compare_fusion, f32[2,6,512]{2,1,0:T(8,128)S(1)} %get-tuple-element.46, bf16[2048,2,128,1]{2,1,0,3:T(2,128)(2,1)S(1)} %bitcast.32), kind=kOutput, calls=%fused_computation.11 | convolution fusion | flops 3284926464 | bytes 55623680 | tf_op jit(solution)/shard_map/cond/branch_0_fun/kqsr,rkd->kqsd/dot_general | solution.py:99
  118.8 3.5 copy.38
  122.3 2.3 divide_convert_fusion
  124.7 15.7 %convolution_convert_fusion = bf16[512,6144]{1,0:T(8,128)(2,1)} fusion(bf16[512,1536]{0,1:T(8,128)(2,1)S(1)} %bitcast.31, bf16[1536,6144]{1,0:T(8,128)(2,1)} %param.18), kind=kOutput, calls=%fused_computation.22 | convolution fusion | flops 9666822144 | bytes 26738688 | tf_op jit(solution)/shard_map/dot_general | solution.py:116
  140.3 0.0 reduce-scatter.3.cloned.1.call-update
  140.4 0.0 copy-start.7
  140.4 0.0 copy-start.5
  140.4 0.0 copy-start.6
  140.4 0.0 all-gather.8.cloned.1.call-start
  140.5 110.8 %reduce-scatter.3.cloned.1.call-done = bf16[512,1536]{1,0:T(8,128)(2,1)} async-done(((bf16[512,6144]{1,0:T(8,128)(2,1)}), bf16[512,1536]{1,0:T(8,128)(2,1)}) %reduce-scatter.3.cloned.1.call-update) | async-done | bytes 1572880 | tf_op jit(solution)/shard_map/reduce_scatter | solution.py:117
  251.3 2.9 add_convert_fusion.1
  254.2 0.0 all-gather.8.cloned.1.call-update
  254.3 0.0 all-reduce.5.cloned.1.call-start
  254.4 0.1 fusion.33
  254.4 46.9 %all-gather.8.cloned.1.call-done = bf16[2048,1536]{1,0:T(8,128)(2,1)} async-done(((bf16[512,1536]{1,0:T(8,128)(2,1)}), bf16[2048,1536]{1,0:T(8,128)(2,1)}) %all-gather.8.cloned.1.call-update) | async-done | bytes 6291472 | tf_op jit(solution)/shard_map/all_gather | solution.py:129
  301.3 11.4 %scatter_custom_fusion = bf16[640,1536]{1,0:T(8,128)(2,1)S(1)} fusion(s32[2048]{0:T(1024)S(1)} %bitcast.35, bf16[2048,1536]{1,0:T(8,128)(2,1)} %all-gather.8.cloned.1.call-done, bf16[]{:T(256)} %constant.48.clone.1), kind=kCustom, calls=%fused_computation.36 | custom fusion | bytes 1966592 | tf_op jit(solution)/shard_map/scatter | solution.py:129
  312.8 8.5 %convolution_convert_fusion.1 = bf16[640,2048]{1,0:T(8,128)(2,1)} fusion(bf16[1536,2048]{1,0:T(8,128)(2,1)} %param.22, bf16[640,1536]{1,0:T(8,128)(2,1)S(1)} %scatter_custom_fusion, f32[1536]{0:T(1024)S(1)} %convert_element_type.85), kind=kOutput, calls=%fused_computation.28 | convolution fusion | flops 4030791680 | bytes 10885120 | tf_op jit(solution)/shard_map/dot_general | solution.py:135
  321.2 8.2 %convolution_convert_fusion.2 = bf16[640,2048]{1,0:T(8,128)(2,1)} fusion(bf16[1536,2048]{1,0:T(8,128)(2,1)} %param.21, bf16[640,1536]{1,0:T(8,128)(2,1)S(1)} %scatter_custom_fusion, f32[1536]{0:T(1024)S(1)} %convert_element_type.85), kind=kOutput, calls=%fused_computation.29 | convolution fusion | flops 4030791680 | bytes 10885120 | tf_op jit(solution)/shard_map/dot_general | solution.py:134
  329.5 0.0 all-reduce.5.cloned.1.call-update
  329.5 0.0 reduce-scatter.5.cloned.1.call-start
  329.6 8.0 %scatter_custom_fusion.1 = s32[640]{0:T(1024)S(1)} fusion(s32[2048]{0:T(1024)S(1)} %bitcast.36, s32[2048]{0:T(1024)S(1)} %get-tuple-element.40, s32[]{:T(128)} %constant.22.clone.1), kind=kCustom, calls=%fused_computation.54 | custom fusion | bytes 2564 | tf_op jit(solution)/shard_map/scatter | solution.py:23
  337.7 0.5 fusion.17
  338.1 0.6 fusion.23
  338.7 19.9 %all-reduce.1 = (bf16[640]{0:T(1024)(128)(2,1)S(1)}, bf16[640,8]{0,1:T(8,128)(2,1)S(1)}) all-reduce(bf16[640]{0:T(1024)(128)(2,1)S(1)} %fusion.17, bf16[640,8]{0,1:T(8,128)(2,1)S(1)} %fusion.23), channel_id=1, replica_groups=mesh['groups'=2,'wide'=4,'ctx'=4] {'wide'}, use_global_device_ids=true, to_apply=%region_9.10 | all-reduce | flops 5760 | bytes 23040 | tf_op jit(solution)/shard_map/psum | solution.py:140
  358.7 160.5 %all-reduce.5.cloned.1.call-done = (bf16[640,2048]{1,0:T(8,128)(2,1)}, bf16[640,2048]{1,0:T(8,128)(2,1)}) async-done(((bf16[640,2048]{1,0:T(8,128)(2,1)}, bf16[640,2048]{1,0:T(8,128)(2,1)}), (bf16[640,2048]{1,0:T(8,128)(2,1)}, bf16[640,2048]{1,0:T(8,128)(2,1)})) %all-reduce.5.cloned.1.call-update) | async-done | bytes 5242896 | tf_op jit(solution)/shard_map/psum | solution.py:139
  519.2 9.2 %fusion.18 = bf16[640,1536]{1,0:T(8,128)(2,1)S(1)} fusion(bf16[2048,1536]{1,0:T(8,128)(2,1)} %param.23, bf16[640,2048]{1,0:T(8,128)(2,1)} %get-tuple-element.44, bf16[640,2048]{1,0:T(8,128)(2,1)} %get-tuple-element.45, f32[640]{0:T(1024)S(1)} %divide_reduce_fusion, f32[640]{0:T(1024)S(1)} %add_rsqrt_fusion), kind=kOutput, calls=%fused_computation.33 | convolution fusion | flops 4040949760 | bytes 13505536 | tf_op jit(solution)/shard_map/dot_general | solution.py:144
  528.4 0.1 concatenate.3
  528.5 10.1 %gather_fusion = bf16[2048,1536]{1,0:T(8,128)(2,1)} fusion(bf16[641,1536]{1,0:T(8,128)(2,1)S(1)} %concatenate.3, s32[2048]{0:T(1024)S(1)} %broadcast_clamp_fusion), kind=kCustom, calls=%fused_computation | custom fusion | bytes 12591104 | tf_op jit(solution)/shard_map/jit(_take)/gather | solution.py:147
  538.7 6.6 %select_convert_fusion = bf16[2048,1536]{1,0:T(8,128)(2,1)} fusion(bf16[2048,1536]{1,0:T(8,128)(2,1)} %gather_fusion, pred[2048]{0:T(1024)(128)(4,1)S(1)} %compare_and_fusion), kind=kLoop, calls=%fused_computation.21 | loop fusion | flops 3145728 | bytes 12584960 | tf_op jit(solution)/shard_map/convert_element_type | solution.py:147
  545.3 0.0 reduce-scatter.5.cloned.1.call-update
  545.3 58.0 %reduce-scatter.5.cloned.1.call-done = bf16[512,1536]{1,0:T(8,128)(2,1)} async-done(((bf16[2048,1536]{1,0:T(8,128)(2,1)}), bf16[512,1536]{1,0:T(8,128)(2,1)}) %reduce-scatter.5.cloned.1.call-update) | async-done | bytes 1572880 | tf_op jit(solution)/shard_map/reduce_scatter | solution.py:146
  603.2 2.9 add_convert_fusion
  (25 shorter events, 0.1 us)
Async XLA Ops:
  6.5 1.2 copy-start
  6.5 21.8 %all-gather.4.cloned.1.call-start = ((), (), s32[]{:S(2)}) async-start(), calls=%async_computation.2 | async-start | bytes 1310720 | tf_op jit(solution)/shard_map/all_gather | solution.py:78
  8.5 38.1 %all-gather.6.cloned.1.call-start = ((), (), s32[]{:S(2)}) async-start(), calls=%async_computation.3 | async-start | bytes 1310720 | tf_op jit(solution)/shard_map/all_gather | solution.py:79
  10.3 241.0 %reduce-scatter.3.cloned.1.call-start = ((), (), s32[]{:S(2)}) async-start(), calls=%async_computation.4 | async-start | bytes 7864320 | tf_op jit(solution)/shard_map/reduce_scatter | solution.py:117
  72.4 22.0 %copy-start.4 = (bf16[2048,256]{1,0:T(8,128)(2,1)S(1)}, bf16[2048,256]{1,0:T(8,128)(2,1)}, u32[]{:S(2)}) copy-start(bf16[2048,256]{1,0:T(8,128)(2,1)} %get-tuple-element.22) | copy-start | bytes 3145732 | tf_op jit(solution)/shard_map/cond
  140.3 111.0 %copy-start.3 = (bf16[512,1536]{1,0:T(8,128)(2,1)S(1)}, bf16[512,1536]{1,0:T(8,128)(2,1)}, u32[]{:S(2)}) copy-start(bf16[512,1536]{1,0:T(8,128)(2,1)} %param.17) | copy-start | bytes 4718596
  140.4 113.9 %copy-start.7 = (bf16[1536]{0:T(1024)(128)(2,1)S(1)}, bf16[1536]{0:T(1024)(128)(2,1)}, u32[]{:S(2)}) copy-start(bf16[1536]{0:T(1024)(128)(2,1)} %param.19) | copy-start | bytes 9220
  140.4 114.0 %copy-start.5 = (s32[2048,2]{0,1:T(2,128)S(1)}, s32[2048,2]{0,1:T(2,128)}, u32[]{:S(2)}) copy-start(s32[2048,2]{0,1:T(2,128)} %param.24) | copy-start | bytes 49156
  140.4 114.0 %copy-start.6 = (s32[2048,2]{0,1:T(2,128)S(1)}, s32[2048,2]{0,1:T(2,128)}, u32[]{:S(2)}) copy-start(s32[2048,2]{0,1:T(2,128)} %param.25) | copy-start | bytes 49156
  140.4 160.9 %all-gather.8.cloned.1.call-start = ((), (), s32[]{:S(2)}) async-start(), calls=%async_computation.5 | async-start | bytes 7864320 | tf_op jit(solution)/shard_map/all_gather | solution.py:129
  254.3 264.9 %all-reduce.5.cloned.1.call-start = ((), (), s32[]{:S(2)}) async-start(), calls=%async_computation.7 | async-start | bytes 10485760 | tf_op jit(solution)/shard_map/psum | solution.py:139
  329.5 8.6 %copy-start.8 = (bf16[1536,8]{0,1:T(8,128)(2,1)S(1)}, bf16[1536,8]{0,1:T(8,128)(2,1)}, u32[]{:S(2)}) copy-start(bf16[1536,8]{0,1:T(8,128)(2,1)} %param.20) | copy-start | bytes 73732
  329.5 273.7 %reduce-scatter.5.cloned.1.call-start = ((), (), s32[]{:S(2)}) async-start(), calls=%async_computation.6 | async-start | bytes 7864320 | tf_op jit(solution)/shard_map/reduce_scatter | solution.py:146
  545.3 58.0 %copy-start.2 = (bf16[512,1536]{1,0:T(8,128)(2,1)S(1)}, bf16[512,1536]{1,0:T(8,128)(2,1)}, u32[]{:S(2)}) copy-start(bf16[512,1536]{1,0:T(8,128)(2,1)} %add_convert_fusion.1) | copy-start | bytes 4718596
  545.3 60.9 %copy-start.1 = (bf16[512,1024]{1,0:T(8,128)(2,1)S(1)}, bf16[512,1024]{1,0:T(8,128)(2,1)}, u32[]{:S(2)}) copy-start(bf16[512,1024]{1,0:T(8,128)(2,1)} %param.15) | copy-start | bytes 3145732
Sparse Core Ops, SparseCore 0:
  8.9 19.4 all-gather.3
  29.9 16.6 all-gather.5
  140.5 110.7 reduce-scatter.2
  254.4 46.8 all-gather.7
  329.6 189.4 all-reduce.4
  545.4 57.7 reduce-scatter.4
where the time goes:
time: 614 us; the launch traced here: 613 us
  waiting for transfers between devices  413 us (67%)
  matrix products  87.4 us (14%)
  local copies, waits for them, and re-layouts  41.1 us (7%)
  other arithmetic  38.2 us (6%)
  blocking collectives  19.9 us (3%)
  between operations  13.6 us (2%)
    psum x1, waiting for transfers between devices, local(): lax.psum(up_part.astype(jnp.bfloat16), 'wide').astype(jnp.float32)  160 us
    reduce_scatter x1, waiting for transfers between devices, local(): lax.psum_scatter(partial_out.astype(jnp.bfloat16), 'wide', scatter_dimens...  111 us
    reduce_scatter x1, waiting for transfers between devices, local(): lax.psum_scatter(jnp.take(expert_pad, slot_of_token, axis=0).astype(jnp.b...  58 us
    all_gather x1, waiting for transfers between devices, local(): lax.all_gather(resid, 'ctx', axis=0, tiled=True)  46.9 us
    dot_general x1, matrix products, update(): jnp.einsum('kqsr,rkd->kqsd', weights.astype(jnp.bfloat16), value_piece, p...  24 us
    reduce_sum x1, other arithmetic, update(): new_sum = running_sum * decay + jnp.sum(weights, axis=-1)  22 us
    dot_general x1, matrix products, update(): jnp.einsum('skqd,rkd->kqsr', query_blocks, key_piece, preferred_element_t...  21.1 us
    psum x1, blocking collectives, local(): lax.psum(square_part.astype(jnp.bfloat16), 'wide').astype(jnp.float32)  19.9 us
  transfers between devices with their start and end apart: 6, of which 6 were waited for; matrix products, arithmetic and copies ran while one was open for 2% of the time, Pallas kernels for 0%

commit v1 on v0

--- a/solution.py
+++ b/solution.py
@@ -10,6 +10,10 @@
 HEAD_SIZE = 128
 NEG_FILL = -1e30
 EPSILON = 1e-05
+
+
+def wait_the_entries(z, shard_axis):
+    return lax.all_gather(z, shard_axis).sum(axis=0)
 
 
 def token_slots(expert_ids, slot_ids, capacity):
@@ -136,7 +140,7 @@
     logit_part = jnp.dot(scaled, router_weight, preferred_element_type=jnp.float32)
     gate_sum, up_sum, square_sum, logit_sum = (
         lax.psum(gate_part.astype(jnp.bfloat16), "wide").astype(jnp.float32),
-        lax.psum(up_part.astype(jnp.bfloat16), "wide").astype(jnp.float32),
+        wait_the_entries(up_part.astype(jnp.bfloat16), "wide").astype(jnp.float32),
         lax.psum(square_part.astype(jnp.bfloat16), "wide").astype(jnp.float32),
         lax.psum(logit_part.astype(jnp.bfloat16), "wide").astype(jnp.float32),
     )

time: 614 us -> 715 us (1.16); the launches traced: 613 us -> 705 us
  waiting for transfers between devices: 413 us -> 487 us
  other arithmetic: 38.2 us -> 46.9 us
  blocking collectives: 19.9 us -> 28.1 us
    all_gather x0 -> x1, waiting for transfers between devices: none -> 139 us  [wait_the_entries(): return lax.all_gather(z, shard_axis).sum(axis=0)]
    psum x1, waiting for transfers between devices: 160 us -> 95.9 us  [local(): lax.psum(gate_part.astype(jnp.bfloat16), 'wide').astype(jnp.float32)]
    reduce_sum x0 -> x1, other arithmetic: none -> 8.71 us  [wait_the_entries(): return lax.all_gather(z, shard_axis).sum(axis=0)]
    psum x1, blocking collectives: 19.9 us -> 28.1 us  [local(): lax.psum(square_part.astype(jnp.bfloat16), 'wide').astype(jnp.float32)]
  transfers between devices with their start and end apart: 6 -> 7, of which waited for: 6 -> 7; matrix products, arithmetic and copies ran while one was open for 2% -> 4% of each run, Pallas kernels for 0% -> 0%
where the time goes in v1:
time: 715 us; the launch traced here: 705 us
  waiting for transfers between devices  487 us (68%)
  matrix products  87.4 us (12%)
  other arithmetic  46.9 us (7%)
  local copies, waits for them, and re-layouts  41.2 us (6%)
  blocking collectives  28.1 us (4%)
  between operations  14 us (2%)
    all_gather x1, waiting for transfers between devices, wait_the_entries(): return lax.all_gather(z, shard_axis).sum(axis=0)  139 us
    reduce_scatter x1, waiting for transfers between devices, local(): lax.psum_scatter(partial_out.astype(jnp.bfloat16), 'wide', scatter_dimens...  111 us
    psum x1, waiting for transfers between devices, local(): lax.psum(gate_part.astype(jnp.bfloat16), 'wide').astype(jnp.float32)  95.9 us
    reduce_scatter x1, waiting for transfers between devices, local(): lax.psum_scatter(jnp.take(expert_pad, slot_of_token, axis=0).astype(jnp.b...  58 us
    all_gather x1, waiting for transfers between devices, local(): lax.all_gather(resid, 'ctx', axis=0, tiled=True)  46.9 us
    psum x1, blocking collectives, local(): lax.psum(square_part.astype(jnp.bfloat16), 'wide').astype(jnp.float32)  28.1 us
    dot_general x1, matrix products, update(): jnp.einsum('kqsr,rkd->kqsd', weights.astype(jnp.bfloat16), value_piece, p...  24.1 us
    reduce_sum x1, other arithmetic, update(): new_sum = running_sum * decay + jnp.sum(weights, axis=-1)  22 us
  transfers between devices with their start and end apart: 7, of which 7 were waited for; matrix products, arithmetic and copies ran while one was open for 4% of the time, Pallas kernels for 0%

profile of v1, /device:TPU:0, one launch (start us, length us, event | category | flops | bytes accessed | tf_op | source)
XLA Modules:
  0.0 704.6 jit_solution(2383391896233256260)
XLA Ops:
  6.5 1.2 copy-done
  7.8 0.7 constant_dynamic-slice_fusion.1
  8.5 0.0 all-gather.6.cloned.1.call-update
  8.5 0.0 all-gather.8.cloned.1.call-start
  8.6 1.7 constant_dynamic-slice_fusion
  10.2 0.0 all-gather.8.cloned.1.call-update
  10.3 0.0 reduce-scatter.3.cloned.1.call-start
  10.3 18.0 %all-gather.6.cloned.1.call-done = bf16[2048,256]{1,0:T(8,128)(2,1)} async-done(((bf16[512,256]{1,0:T(8,128)(2,1)}), bf16[2048,256]{1,0:T(8,128)(2,1)}) %all-gather.6.cloned.1.call-update) | async-done | bytes 1048592 | tf_op jit(solution)/shard_map/all_gather | solution.py:82
  28.3 18.3 %all-gather.8.cloned.1.call-done = bf16[2048,256]{1,0:T(8,128)(2,1)} async-done(((bf16[512,256]{1,0:T(8,128)(2,1)}), bf16[2048,256]{1,0:T(8,128)(2,1)}) %all-gather.8.cloned.1.call-update) | async-done | bytes 1048592 | tf_op jit(solution)/shard_map/all_gather | solution.py:83
  46.6 75.8 %conditional.1 = (f32[2,6,512]{2,1,0:T(8,128)S(1)}, f32[2,6,512,128]{2,3,1,0:T(8,128)}) conditional(s32[]{:T(128)} %convert_element_type.78, (s32[]{:T(128)}, s32[512]{0:T(512)S(1)}, bf16[2048,256]{1,0:T(8,128)(2,1)}, bf16[512,1536]{1,0:T(8,128)(2,1)}, bf16[2048,256]{1,0:T(8,128)(2,1)}) %tuple.13, () %tuple.14), branch_computations={%region_0.3_spmd, %region_3.4_spmd} | conditional | flops 6607870464 | bytes 180058160 | solution.py:111
  46.6 0.8 iota_compare_fusion
  47.5 1.7 copy.28
  49.2 2.1 reshape.71
  51.3 21.1 %fusion = (f32[2,6,512]{2,1,0:T(8,128)S(1)}, f32[2,2048,512,6]{2,1,3,0:T(8,128)}) fusion(pred[512,2048]{0,1:T(8,128)(4,1)S(1)} %iota_compare_fusion, bf16[512,2,6,128]{0,3,2,1:T(8,128)(2,1)S(1)} %bitcast.31, bf16[2048,2,128,1]{2,1,0,3:T(2,128)(2,1)} %bitcast.32), kind=kOutput, calls=%fused_computation.5 | convolution fusion | flops 3258968064 | bytes 54026240 | tf_op jit(solution)/shard_map/cond/branch_0_fun/skqd,rkd->kqsr/dot_general | solution.py:91
  72.5 22.0 %fusion.2 = f32[2,6,512]{2,1,0:T(8,128)S(1)} fusion(f32[2,2048,512,6]{2,1,3,0:T(8,128)} %get-tuple-element.47, f32[2,6,512]{2,1,0:T(8,128)S(1)} %get-tuple-element.46, pred[512,2048]{0,1:T(8,128)(4,1)S(1)} %iota_compare_fusion), kind=kLoop, calls=%fused_computation.7 | loop fusion | flops 62908416 | bytes 51429376 | tf_op jit(solution)/shard_map/cond/branch_0_fun/reduce_sum | solution.py:102
  94.4 0.3 reshape.73
  94.7 24.1 %fusion.6 = f32[2,6,512,128]{3,2,1,0:T(8,128)} fusion(f32[2,2048,512,6]{2,1,3,0:T(8,128)} %get-tuple-element.47, f32[2,6,512]{2,1,0:T(8,128)S(1)} %get-tuple-element.46, pred[512,2048]{0,1:T(8,128)(4,1)S(1)} %iota_compare_fusion, f32[2,6,512]{2,1,0:T(8,128)S(1)} %get-tuple-element.44, bf16[2048,2,128,1]{2,1,0,3:T(2,128)(2,1)S(1)} %bitcast.34), kind=kOutput, calls=%fused_computation.11 | convolution fusion | flops 3284926464 | bytes 55623680 | tf_op jit(solution)/shard_map/cond/branch_0_fun/kqsr,rkd->kqsd/dot_general | solution.py:103
  118.8 3.7 copy.38
  122.5 2.3 divide_convert_fusion
  124.8 15.7 %convolution_convert_fusion = bf16[512,6144]{1,0:T(8,128)(2,1)} fusion(bf16[512,1536]{0,1:T(8,128)(2,1)S(1)} %bitcast.33, bf16[1536,6144]{1,0:T(8,128)(2,1)} %param.18), kind=kOutput, calls=%fused_computation.22 | convolution fusion | flops 9666822144 | bytes 26738688 | tf_op jit(solution)/shard_map/dot_general | solution.py:120
  140.5 0.0 reduce-scatter.3.cloned.1.call-update
  140.6 0.0 all-gather.10.cloned.1.call-start
  140.6 110.8 %reduce-scatter.3.cloned.1.call-done = bf16[512,1536]{1,0:T(8,128)(2,1)} async-done(((bf16[512,6144]{1,0:T(8,128)(2,1)}), bf16[512,1536]{1,0:T(8,128)(2,1)}) %reduce-scatter.3.cloned.1.call-update) | async-done | bytes 1572880 | tf_op jit(solution)/shard_map/reduce_scatter | solution.py:121
  251.5 2.9 add_convert_fusion.1
  254.4 0.0 all-gather.10.cloned.1.call-update
  254.4 0.0 all-gather.12.cloned.1.call-start
  254.5 0.1 fusion.33
  254.6 46.9 %all-gather.10.cloned.1.call-done = bf16[2048,1536]{1,0:T(8,128)(2,1)} async-done(((bf16[512,1536]{1,0:T(8,128)(2,1)}), bf16[2048,1536]{1,0:T(8,128)(2,1)}) %all-gather.10.cloned.1.call-update) | async-done | bytes 6291472 | tf_op jit(solution)/shard_map/all_gather | solution.py:133
  301.5 11.4 %scatter_custom_fusion = bf16[640,1536]{1,0:T(8,128)(2,1)S(1)} fusion(s32[2048]{0:T(1024)S(1)} %bitcast.37, bf16[2048,1536]{1,0:T(8,128)(2,1)} %all-gather.10.cloned.1.call-done, bf16[]{:T(256)} %constant.49.clone.1), kind=kCustom, calls=%fused_computation.36 | custom fusion | bytes 1966592 | tf_op jit(solution)/shard_map/scatter | solution.py:133
  312.9 8.3 %convolution_convert_fusion.1 = bf16[640,2048]{1,0:T(8,128)(2,1)} fusion(bf16[1536,2048]{1,0:T(8,128)(2,1)} %param.22, bf16[640,1536]{1,0:T(8,128)(2,1)S(1)} %scatter_custom_fusion, f32[1536]{0:T(1024)S(1)} %convert_element_type.87), kind=kOutput, calls=%fused_computation.28 | convolution fusion | flops 4030791680 | bytes 10885120 | tf_op jit(solution)/shard_map/dot_general | solution.py:139
  321.2 0.0 all-gather.12.cloned.1.call-update
  321.2 0.0 all-reduce.4.cloned.1.call-start
  321.3 8.5 %convolution_convert_fusion.2 = bf16[640,2048]{1,0:T(8,128)(2,1)} fusion(bf16[1536,2048]{1,0:T(8,128)(2,1)} %param.21, bf16[640,1536]{1,0:T(8,128)(2,1)S(1)} %scatter_custom_fusion, f32[1536]{0:T(1024)S(1)} %convert_element_type.87), kind=kOutput, calls=%fused_computation.29 | convolution fusion | flops 4030791680 | bytes 10885120 | tf_op jit(solution)/shard_map/dot_general | solution.py:138
  329.8 0.0 all-reduce.4.cloned.1.call-update
  329.8 0.0 reduce-scatter.5.cloned.1.call-start
  329.8 8.0 %scatter_custom_fusion.1 = s32[640]{0:T(1024)S(1)} fusion(s32[2048]{0:T(1024)S(1)} %bitcast.38, s32[2048]{0:T(1024)S(1)} %get-tuple-element.40, s32[]{:T(128)} %constant.23.clone.1), kind=kCustom, calls=%fused_computation.54 | custom fusion | bytes 2564 | tf_op jit(solution)/shard_map/scatter | solution.py:27
  337.9 0.5 fusion.17
  338.4 0.6 fusion.23
  339.0 28.1 %all-reduce.1 = (bf16[640]{0:T(1024)(128)(2,1)S(1)}, bf16[640,8]{0,1:T(8,128)(2,1)S(1)}) all-reduce(bf16[640]{0:T(1024)(128)(2,1)S(1)} %fusion.17, bf16[640,8]{0,1:T(8,128)(2,1)S(1)} %fusion.23), channel_id=1, replica_groups=mesh['groups'=2,'wide'=4,'ctx'=4] {'wide'}, use_global_device_ids=true, to_apply=%region_9.10 | all-reduce | flops 5760 | bytes 23040 | tf_op jit(solution)/shard_map/psum | solution.py:144
  367.2 138.6 %all-gather.12.cloned.1.call-done = bf16[2560,2048]{1,0:T(8,128)(2,1)} async-done(((bf16[640,2048]{1,0:T(8,128)(2,1)}), bf16[2560,2048]{1,0:T(8,128)(2,1)}) %all-gather.12.cloned.1.call-update) | async-done | bytes 10485776 | tf_op jit(solution)/shard_map/all_gather | solution.py:16
  505.8 8.7 %reduce_sum.51 = bf16[640,2048]{1,0:T(8,128)(2,1)} reduce(bf16[4,640,2048]{2,1,0:T(8,128)(2,1)} %bitcast.30, bf16[]{:T(256)} %constant.49.clone.1), dimensions={0}, to_apply=%region_10.11 | reduce | flops 3932160 | bytes 13107202 | tf_op jit(solution)/shard_map/reduce_sum | solution.py:16
  514.5 95.9 %all-reduce.4.cloned.1.call-done = bf16[640,2048]{1,0:T(8,128)(2,1)} async-done(((bf16[640,2048]{1,0:T(8,128)(2,1)}), bf16[640,2048]{1,0:T(8,128)(2,1)}) %all-reduce.4.cloned.1.call-update) | async-done | bytes 2621456 | tf_op jit(solution)/shard_map/psum | solution.py:142
  610.3 9.2 %fusion.18 = bf16[640,1536]{1,0:T(8,128)(2,1)S(1)} fusion(bf16[2048,1536]{1,0:T(8,128)(2,1)} %param.23, bf16[640,2048]{1,0:T(8,128)(2,1)} %reduce_sum.51, bf16[640,2048]{1,0:T(8,128)(2,1)} %all-reduce.4.cloned.1.call-done, f32[640]{0:T(1024)S(1)} %divide_reduce_fusion, f32[640]{0:T(1024)S(1)} %add_rsqrt_fusion), kind=kOutput, calls=%fused_computation.33 | convolution fusion | flops 4040949760 | bytes 13505536 | tf_op jit(solution)/shard_map/dot_general | solution.py:148
  619.6 0.1 concatenate.3
  619.7 10.1 %gather_fusion = bf16[2048,1536]{1,0:T(8,128)(2,1)} fusion(bf16[641,1536]{1,0:T(8,128)(2,1)S(1)} %concatenate.3, s32[2048]{0:T(1024)S(1)} %broadcast_clamp_fusion), kind=kCustom, calls=%fused_computation | custom fusion | bytes 12591104 | tf_op jit(solution)/shard_map/jit(_take)/gather | solution.py:151
  629.8 6.6 select_convert_fusion
  636.4 58.0 %reduce-scatter.5.cloned.1.call-done = bf16[512,1536]{1,0:T(8,128)(2,1)} async-done(((bf16[2048,1536]{1,0:T(8,128)(2,1)}), bf16[512,1536]{1,0:T(8,128)(2,1)}) %reduce-scatter.5.cloned.1.call-update) | async-done | bytes 1572880 | tf_op jit(solution)/shard_map/reduce_scatter | solution.py:150
  694.4 2.9 add_convert_fusion
  (29 shorter events, 0.2 us)
Async XLA Ops:
  6.5 1.2 copy-start
  6.5 21.8 %all-gather.6.cloned.1.call-start = ((), (), s32[]{:S(2)}) async-start(), calls=%async_computation.2 | async-start | bytes 1310720 | tf_op jit(solution)/shard_map/all_gather | solution.py:82
  8.5 38.1 %all-gather.8.cloned.1.call-start = ((), (), s32[]{:S(2)}) async-start(), calls=%async_computation.3 | async-start | bytes 1310720 | tf_op jit(solution)/shard_map/all_gather | solution.py:83
  10.3 241.2 %reduce-scatter.3.cloned.1.call-start = ((), (), s32[]{:S(2)}) async-start(), calls=%async_computation.4 | async-start | bytes 7864320 | tf_op jit(solution)/shard_map/reduce_scatter | solution.py:121
  72.4 22.0 %copy-start.4 = (bf16[2048,256]{1,0:T(8,128)(2,1)S(1)}, bf16[2048,256]{1,0:T(8,128)(2,1)}, u32[]{:S(2)}) copy-start(bf16[2048,256]{1,0:T(8,128)(2,1)} %get-tuple-element.22) | copy-start | bytes 3145732 | tf_op jit(solution)/shard_map/cond
  140.5 111.0 %copy-start.3 = (bf16[512,1536]{1,0:T(8,128)(2,1)S(1)}, bf16[512,1536]{1,0:T(8,128)(2,1)}, u32[]{:S(2)}) copy-start(bf16[512,1536]{1,0:T(8,128)(2,1)} %param.17) | copy-start | bytes 4718596
  140.5 113.9 %copy-start.7 = (bf16[1536]{0:T(1024)(128)(2,1)S(1)}, bf16[1536]{0:T(1024)(128)(2,1)}, u32[]{:S(2)}) copy-start(bf16[1536]{0:T(1024)(128)(2,1)} %param.19) | copy-start | bytes 9220
  140.5 114.0 %copy-start.5 = (s32[2048,2]{0,1:T(2,128)S(1)}, s32[2048,2]{0,1:T(2,128)}, u32[]{:S(2)}) copy-start(s32[2048,2]{0,1:T(2,128)} %param.24) | copy-start | bytes 49156
  140.6 113.9 %copy-start.6 = (s32[2048,2]{0,1:T(2,128)S(1)}, s32[2048,2]{0,1:T(2,128)}, u32[]{:S(2)}) copy-start(s32[2048,2]{0,1:T(2,128)} %param.25) | copy-start | bytes 49156
  140.6 160.9 %all-gather.10.cloned.1.call-start = ((), (), s32[]{:S(2)}) async-start(), calls=%async_computation.5 | async-start | bytes 7864320 | tf_op jit(solution)/shard_map/all_gather | solution.py:133
  254.4 251.3 %all-gather.12.cloned.1.call-start = ((), (), s32[]{:S(2)}) async-start(), calls=%async_computation.8 | async-start | bytes 13107200 | tf_op jit(solution)/shard_map/all_gather | solution.py:16
  321.2 289.1 %all-reduce.4.cloned.1.call-start = ((), (), s32[]{:S(2)}) async-start(), calls=%async_computation.6 | async-start | bytes 5242880 | tf_op jit(solution)/shard_map/psum | solution.py:142
  329.8 8.6 %copy-start.8 = (bf16[1536,8]{0,1:T(8,128)(2,1)S(1)}, bf16[1536,8]{0,1:T(8,128)(2,1)}, u32[]{:S(2)}) copy-start(bf16[1536,8]{0,1:T(8,128)(2,1)} %param.20) | copy-start | bytes 73732
  329.8 364.7 %reduce-scatter.5.cloned.1.call-start = ((), (), s32[]{:S(2)}) async-start(), calls=%async_computation.7 | async-start | bytes 7864320 | tf_op jit(solution)/shard_map/reduce_scatter | solution.py:150
  636.4 58.0 %copy-start.2 = (bf16[512,1536]{1,0:T(8,128)(2,1)S(1)}, bf16[512,1536]{1,0:T(8,128)(2,1)}, u32[]{:S(2)}) copy-start(bf16[512,1536]{1,0:T(8,128)(2,1)} %add_convert_fusion.1) | copy-start | bytes 4718596
  636.4 61.0 %copy-start.1 = (bf16[512,1024]{1,0:T(8,128)(2,1)S(1)}, bf16[512,1024]{1,0:T(8,128)(2,1)}, u32[]{:S(2)}) copy-start(bf16[512,1024]{1,0:T(8,128)(2,1)} %param.15) | copy-start | bytes 3145732
Sparse Core Ops, SparseCore 0:
  8.9 19.4 all-gather.5
  29.9 16.6 all-gather.7
  140.7 110.7 reduce-scatter.2
  254.5 46.8 all-gather.9
  321.3 184.3 all-gather.11
  508.0 102.2 all-reduce.3
  636.5 57.8 reduce-scatter.4
